TPU v7x, 128 devices: a whole 4x4x4 slice. The times are simulated.
128 devices in a mesh: rep: 8 (over z_hi, x), shard: 16 (over y, z_lo, core).
Axes of the slice: x: 4, y: 4, z: 4 (z_hi: 2, z_lo: 2; z = z_hi * 2 + z_lo), core: 2. Of those that a mesh axis runs over, the one named last changes fastest.
Arguments:
- inner_wqkv: float32 [8, 2048, 4096], P('rep', 'shard'), may hold values from -8.5 to 8.5
- inner_w1: float32 [8, 2048, 6144], P('rep', 'shard'), may hold values from -8.5 to 8.5
- inner_w3: float32 [8, 2048, 6144], P('rep', 'shard'), may hold values from -8.5 to 8.5
- inner_wo: float32 [8, 2048, 2048], P('rep', 'shard'), may hold values from -8.5 to 8.5
- inner_w2: float32 [8, 6144, 2048], P('rep', 'shard'), may hold values from -8.5 to 8.5
- outer_wqkv: float32 [2048, 4096], P('shard', 'rep'), may hold values from -8 to 8
- outer_w1: float32 [2048, 6144], P('shard', 'rep'), may hold values from -8 to 8
- outer_w3: float32 [2048, 6144], P('shard', 'rep'), may hold values from -8 to 8
- outer_wo: float32 [2048, 2048], P('shard', 'rep'), may hold values from -8 to 8
- outer_w2: float32 [6144, 2048], P('shard', 'rep'), may hold values from -8 to 8
- moment_wqkv: float32 [2048, 4096], P('shard', 'rep'), may hold values from -0.4 to 0.4
- moment_w1: float32 [2048, 6144], P('shard', 'rep'), may hold values from -0.4 to 0.4
- moment_w3: float32 [2048, 6144], P('shard', 'rep'), may hold values from -0.4 to 0.4
- moment_wo: float32 [2048, 2048], P('shard', 'rep'), may hold values from -0.4 to 0.4
- moment_w2: float32 [6144, 2048], P('shard', 'rep'), may hold values from -0.4 to 0.4
- basis_wo: float32 [2048, 64], P('shard'), may hold values from -0.5 to 0.5
- basis_w2: float32 [6144, 64], P('shard'), may hold values from -0.3125 to 0.3125
Outputs:
- weights_wqkv: bfloat16 [2048, 4096], P('shard')
- weights_w1: bfloat16 [2048, 6144], P('shard')
- weights_w3: bfloat16 [2048, 6144], P('shard')
- weights_wo: bfloat16 [2048, 2048], P('shard')
- weights_w2: bfloat16 [6144, 2048], P('shard')
- master_wqkv: float32 [2048, 4096], P('shard', 'rep')
- master_w1: float32 [2048, 6144], P('shard', 'rep')
- master_w3: float32 [2048, 6144], P('shard', 'rep')
- master_wo: float32 [2048, 2048], P('shard', 'rep')
- master_w2: float32 [6144, 2048], P('shard', 'rep')
- momentum_wqkv: float32 [2048, 4096], P('shard', 'rep')
- momentum_w1: float32 [2048, 6144], P('shard', 'rep')
- momentum_w3: float32 [2048, 6144], P('shard', 'rep')
- momentum_wo: float32 [2048, 2048], P('shard', 'rep')
- momentum_w2: float32 [6144, 2048], P('shard', 'rep')
All inputs are finite; a program needn't handle non-finite values.
Results may differ from a plain program's by a relative error of at most 0.007.
Values may be sent and summed in bfloat16 or wider, within the bound.
No kernel may reach another device: no remote copies, remote signals or barrier semaphores. Data moves between devices by JAX's collectives and lax.ppermute only.
A program may use at most 128 MiB of HBM per device.

v0:
```python
import jax
import jax.numpy as jnp
from jax import lax
from jax.sharding import PartitionSpec as P

rate_outer = 0.7
decay_moment = 0.9


def project(basis, matrix):
    return lax.dot_general(
        basis,
        matrix,
        (((0,), (0,)), ((), ())),
        precision=lax.Precision.HIGHEST,
        preferred_element_type=jnp.float32,
    )


def rebuild(basis, coeff):
    return jnp.dot(
        basis, coeff, precision=lax.Precision.HIGHEST, preferred_element_type=jnp.float32
    )


def nesterov(outer, moment, delta):
    moment_new = decay_moment * moment + delta
    master = outer - rate_outer * (delta + decay_moment * moment_new)
    return (master.astype(jnp.bfloat16), master, moment_new)


def by_owner(a, n):
    r, c = a.shape
    return a.reshape(r, n, c // n).transpose(1, 0, 2)


def from_owners(g):
    n, r, w = g.shape
    return g.transpose(1, 0, 2).reshape(r, n * w)


def gather_rep(y, n):
    return lax.all_to_all(jnp.broadcast_to(y[None], (n,) + y.shape), "rep", 0, 0, tiled=True)


def on_device(
    inner_wqkv,
    inner_w1,
    inner_w3,
    inner_wo,
    inner_w2,
    outer_wqkv,
    outer_w1,
    outer_w3,
    outer_wo,
    outer_w2,
    moment_wqkv,
    moment_w1,
    moment_w3,
    moment_wo,
    moment_w2,
    basis_wo,
    basis_w2,
):
    n = lax.axis_size("rep")
    w_qkv = outer_wqkv.shape[1]
    w_ff = outer_w1.shape[1]
    w_o = outer_wo.shape[1]
    w_2 = outer_w2.shape[1]
    rows = inner_wqkv.shape[1]
    rank = basis_wo.shape[1]
    width = w_qkv + 2 * w_ff
    coef_part = jnp.concatenate(
        [by_owner(project(basis_wo, inner_wo[0]), n), by_owner(project(basis_w2, inner_w2[0]), n)],
        axis=2,
    )
    dense = jnp.concatenate(
        [by_owner(inner_wqkv[0], n), by_owner(inner_w1[0], n), by_owner(inner_w3[0], n)], axis=2
    )
    send = jnp.concatenate([dense, coef_part.reshape(n, -1, width)], axis=1)
    total = jnp.sum(lax.all_to_all(send, "rep", 0, 0, tiled=True), axis=0)
    summed = total[:rows]
    own = jnp.concatenate([project(basis_wo, outer_wo), project(basis_w2, outer_w2)], axis=1)
    coeff = lax.psum(own - total[rows:].reshape(rank, w_o + w_2) / n, "shard")
    d_qkv = outer_wqkv - summed[:, :w_qkv] / n
    d_one = outer_w1 - summed[:, w_qkv : w_qkv + w_ff] / n
    d_three = outer_w3 - summed[:, w_qkv + w_ff :] / n
    a0, b0, c0 = nesterov(outer_wqkv, moment_wqkv, d_qkv)
    a1, b1, c1 = nesterov(outer_w1, moment_w1, d_one)
    a3, b3, c3 = nesterov(outer_w3, moment_w3, d_three)
    dense_w = gather_rep(jnp.concatenate([a0, a1, a3], axis=1), n)
    d_out = rebuild(basis_wo, coeff[:, :w_o])
    d_down = rebuild(basis_w2, coeff[:, w_o:])
    ao, bo, co = nesterov(outer_wo, moment_wo, d_out)
    a2, b2, c2 = nesterov(outer_w2, moment_w2, d_down)
    low_w = gather_rep(jnp.concatenate([ao, a2.reshape(rows, -1)], axis=1), n)
    weights_wqkv = from_owners(dense_w[:, :, :w_qkv])
    weights_w1 = from_owners(dense_w[:, :, w_qkv : w_qkv + w_ff])
    weights_w3 = from_owners(dense_w[:, :, w_qkv + w_ff :])
    weights_wo = from_owners(low_w[:, :, :w_o])
    weights_w2 = from_owners(low_w[:, :, w_o:].reshape(n, -1, w_2))
    return (
        weights_wqkv,
        weights_w1,
        weights_w3,
        weights_wo,
        weights_w2,
        b0,
        b1,
        b3,
        bo,
        b2,
        c0,
        c1,
        c3,
        co,
        c2,
    )


def solution(mesh):
    return jax.shard_map(
        on_device,
        mesh=mesh,
        in_specs=(
            P("rep", "shard", None),
            P("rep", "shard", None),
            P("rep", "shard", None),
            P("rep", "shard", None),
            P("rep", "shard", None),
            P("shard", "rep"),
            P("shard", "rep"),
            P("shard", "rep"),
            P("shard", "rep"),
            P("shard", "rep"),
            P("shard", "rep"),
            P("shard", "rep"),
            P("shard", "rep"),
            P("shard", "rep"),
            P("shard", "rep"),
            P("shard", None),
            P("shard", None),
        ),
        out_specs=(
            P("shard", None),
            P("shard", None),
            P("shard", None),
            P("shard", None),
            P("shard", None),
            P("shard", "rep"),
            P("shard", "rep"),
            P("shard", "rep"),
            P("shard", "rep"),
            P("shard", "rep"),
            P("shard", "rep"),
            P("shard", "rep"),
            P("shard", "rep"),
            P("shard", "rep"),
            P("shard", "rep"),
        ),
        check_vma=False,
    )
```

profile of v0, /device:TPU:126, one launch (start us, length us, event | category | flops | bytes accessed | tf_op | source)
XLA Modules:
  0.0 455.8 jit_solution(16131179294469617486)
XLA Ops:
  7.2 2.4 copy.97
  9.6 2.5 copy.96
  12.2 3.2 convolution_bitcast_fusion
  15.4 1.2 convolution_bitcast_fusion.1
  16.8 0.5 reshape.63
  17.3 4.6 %copy.75 = f32[8,16,2048]{1,2,0:T(8,128)} copy(f32[8,16,2048]{2,1,0:T(8,128)S(1)} %reshape.63) | data formatting | bytes 2097152 | tf_op jit(solution)/shard_map/reshape | solution.py:80
  21.9 2.4 copy.71
  24.3 3.6 copy.72
  27.9 3.0 copy.70
  30.9 10.6 %pad_maximum_fusion = f32[8,144,2048]{1,2,0:T(8,128)} fusion(f32[8,16,2048]{1,2,0:T(8,128)} %copy.75, f32[8,128,768]{1,2,0:T(8,128)} %bitcast.55, f32[8,128,768]{1,2,0:T(8,128)S(1)} %bitcast.54, f32[8,128,512]{1,2,0:T(8,128)} %bitcast.57), kind=kLoop, calls=%fused_computation | loop fusion | flops 7077888 | bytes 18874368 | tf_op jit(solution)/shard_map/concatenate | solution.py:80
  41.4 14.7 %copy.76 = f32[8,144,2048]{2,1,0:T(8,128)} copy(f32[8,144,2048]{1,2,0:T(8,128)} %pad_maximum_fusion) | data formatting | bytes 18874368 | tf_op jit(solution)/shard_map/concatenate | solution.py:80
  56.2 7.3 %all-to-all-start = ((f32[8,144,2048]{2,1,0:T(8,128)}), f32[8,144,2048]{2,1,0:T(8,128)}, u32[]{:S(2)}, u32[]{:S(2)}) async-start(f32[8,144,2048]{2,1,0:T(8,128)} %copy.76), calls=%async_computation | async-start | bytes 18874368 | tf_op jit(solution)/shard_map/all_to_all | solution.py:81
  63.5 0.2 fusion.13
  63.7 0.3 fusion.14
  64.1 139.2 %all-to-all-done = f32[8,144,2048]{2,1,0:T(8,128)} async-done(((f32[8,144,2048]{2,1,0:T(8,128)}), f32[8,144,2048]{2,1,0:T(8,128)}, u32[]{:S(2)}, u32[]{:S(2)}) %all-to-all-start) | async-done | bytes 9437216 | tf_op jit(solution)/shard_map/all_to_all | solution.py:81
  203.3 4.7 %reduce_sum.9 = f32[144,2048]{1,0:T(8,128)S(1)} reduce(f32[8,144,2048]{2,1,0:T(8,128)} %all-to-all-done, f32[]{:T(128)} %constant.4.clone.1), dimensions={0}, to_apply=%region_0.0 | reduce | flops 2064384 | bytes 10616836 | tf_op jit(solution)/shard_map/reduce_sum | solution.py:81
  208.1 0.7 maximum_subtract_fusion
  208.8 0.2 copy.83
  209.0 0.2 copy.82
  209.3 114.5 %all-reduce.2.cloned.1.call-done = f32[64,512]{1,0:T(8,128)} async-done(((f32[64,512]{1,0:T(8,128)}), f32[64,512]{1,0:T(8,128)}) %all-reduce.2.cloned.1.call-update) | async-done | bytes 131088 | tf_op jit(solution)/shard_map/psum | solution.py:84
  323.9 2.3 fusion.8
  326.1 0.1 copy.84
  326.4 1.9 fusion.7
  328.4 1.6 broadcast_in_dim.5
  330.0 7.2 %all-to-all-start.2 = ((bf16[8,128,1024]{2,1,0:T(8,128)(2,1)}), bf16[8,128,1024]{2,1,0:T(8,128)(2,1)S(1)}, u32[]{:S(2)}, u32[]{:S(2)}) async-start(bf16[8,128,1024]{2,1,0:T(8,128)(2,1)} %broadcast_in_dim.5), calls=%async_computation.2 | async-start | bytes 4194304 | tf_op jit(solution)/shard_map/all_to_all | solution.py:43
  337.2 1.9 fusion.9
  339.2 2.6 fusion.10
  341.8 19.5 %all-to-all-done.2 = bf16[8,128,1024]{2,1,0:T(8,128)(2,1)S(1)} async-done(((bf16[8,128,1024]{2,1,0:T(8,128)(2,1)}), bf16[8,128,1024]{2,1,0:T(8,128)(2,1)S(1)}, u32[]{:S(2)}, u32[]{:S(2)}) %all-to-all-start.2) | async-done | bytes 2097184 | tf_op jit(solution)/shard_map/all_to_all | solution.py:43
  361.3 2.5 broadcast_in_dim.4
  363.9 10.0 %all-to-all-start.1 = ((bf16[8,128,2048]{2,1,0:T(8,128)(2,1)}), bf16[8,128,2048]{2,1,0:T(8,128)(2,1)}, u32[]{:S(2)}, u32[]{:S(2)}) async-start(bf16[8,128,2048]{2,1,0:T(8,128)(2,1)} %broadcast_in_dim.4), calls=%async_computation.1 | async-start | bytes 8388608 | tf_op jit(solution)/shard_map/all_to_all | solution.py:43
  373.9 0.9 copy.93
  374.8 0.9 copy.95
  375.7 0.8 copy.92
  376.5 0.8 copy.94
  377.2 1.3 slice.58
  378.5 3.7 reshape.69
  382.2 2.8 copy.102
  385.1 0.3 copy.101
  385.3 1.0 copy.91
  386.4 50.1 %all-to-all-done.1 = bf16[8,128,2048]{2,1,0:T(8,128)(2,1)} async-done(((bf16[8,128,2048]{2,1,0:T(8,128)(2,1)}), bf16[8,128,2048]{2,1,0:T(8,128)(2,1)}, u32[]{:S(2)}, u32[]{:S(2)}) %all-to-all-start.1) | async-done | bytes 4194336 | tf_op jit(solution)/shard_map/all_to_all | solution.py:43
  436.4 3.3 fusion.12
  439.7 1.9 copy.99
  441.6 1.6 copy.89
  443.2 0.9 copy.100
  444.1 1.6 copy.90
  445.7 1.3 slice.51
  447.0 0.7 copy.98
  447.7 1.3 copy.88
  (32 shorter events, 0.8 us)
Async XLA Ops:
  7.2 5.0 %copy-start = (f32[384,64]{0,1:T(8,128)S(1)}, f32[384,64]{0,1:T(8,128)}, u32[]{:S(2)}) copy-start(f32[384,64]{0,1:T(8,128)} %param.33) | copy-start | bytes 294916
  9.6 5.8 %copy-start.8 = (f32[128,64]{0,1:T(8,128)S(1)}, f32[128,64]{0,1:T(8,128)}, u32[]{:S(2)}) copy-start(f32[128,64]{0,1:T(8,128)} %param.32) | copy-start | bytes 98308
  12.2 3.2 copy-start.1
  56.2 7.3 %copy-start.5 = (f32[128,256]{1,0:T(8,128)S(1)}, f32[128,256]{1,0:T(8,128)}, u32[]{:S(2)}) copy-start(f32[128,256]{1,0:T(8,128)} %param.25) | copy-start | bytes 393220
  56.2 7.5 %copy-start.2 = (f32[384,256]{1,0:T(8,128)S(1)}, f32[384,256]{1,0:T(8,128)}, u32[]{:S(2)}) copy-start(f32[384,256]{1,0:T(8,128)} %param.26) | copy-start | bytes 1179652
  56.2 147.1 %all-to-all-start = ((f32[8,144,2048]{2,1,0:T(8,128)}), f32[8,144,2048]{2,1,0:T(8,128)}, u32[]{:S(2)}, u32[]{:S(2)}) async-start(f32[8,144,2048]{2,1,0:T(8,128)} %copy.76), calls=%async_computation | async-start | bytes 18874368 | tf_op jit(solution)/shard_map/all_to_all | solution.py:81
  63.5 260.3 %all-reduce.2.cloned.1.call-start = ((), (), s32[]{:S(2)}) async-start(), calls=%async_computation.3 | async-start | bytes 262144 | tf_op jit(solution)/shard_map/psum | solution.py:84
  64.1 145.0 %copy-start.7 = (f32[384,256]{1,0:T(8,128)S(1)}, f32[384,256]{1,0:T(8,128)}, u32[]{:S(2)}) copy-start(f32[384,256]{1,0:T(8,128)} %param.31) | copy-start | bytes 1179652
  64.1 145.1 %copy-start.9 = (f32[128,256]{1,0:T(8,128)S(1)}, f32[128,256]{1,0:T(8,128)}, u32[]{:S(2)}) copy-start(f32[128,256]{1,0:T(8,128)} %param.30) | copy-start | bytes 393220
  330.0 31.3 %all-to-all-start.2 = ((bf16[8,128,1024]{2,1,0:T(8,128)(2,1)}), bf16[8,128,1024]{2,1,0:T(8,128)(2,1)S(1)}, u32[]{:S(2)}, u32[]{:S(2)}) async-start(bf16[8,128,1024]{2,1,0:T(8,128)(2,1)} %broadcast_in_dim.5), calls=%async_computation.2 | async-start | bytes 4194304 | tf_op jit(solution)/shard_map/all_to_all | solution.py:43
  363.9 10.0 %copy-start.4 = (f32[384,256]{0,1:T(8,128)S(1)}, f32[384,256]{0,1:T(8,128)}, u32[]{:S(2)}) copy-start(f32[384,256]{0,1:T(8,128)} %get-tuple-element.78) | copy-start | bytes 1179652
  363.9 10.9 %copy-start.3 = (f32[384,256]{0,1:T(8,128)S(1)}, f32[384,256]{0,1:T(8,128)}, u32[]{:S(2)}) copy-start(f32[384,256]{0,1:T(8,128)} %get-tuple-element.93) | copy-start | bytes 1179652
  363.9 11.8 %copy-start.6 = (f32[128,256]{0,1:T(8,128)S(1)}, f32[128,256]{0,1:T(8,128)}, u32[]{:S(2)}) copy-start(f32[128,256]{0,1:T(8,128)} %get-tuple-element.76) | copy-start | bytes 393220
  363.9 72.6 %all-to-all-start.1 = ((bf16[8,128,2048]{2,1,0:T(8,128)(2,1)}), bf16[8,128,2048]{2,1,0:T(8,128)(2,1)}, u32[]{:S(2)}, u32[]{:S(2)}) async-start(bf16[8,128,2048]{2,1,0:T(8,128)(2,1)} %broadcast_in_dim.4), calls=%async_computation.1 | async-start | bytes 8388608 | tf_op jit(solution)/shard_map/all_to_all | solution.py:43
Sparse Core Ops, SparseCore 0:
  208.9 114.9 all-reduce.1
where the time goes:
time: 457 us; the launch traced here: 456 us
  waiting for transfers between devices  323 us (71%)
  local copies, waits for them, and re-layouts  63.8 us (14%)
  starting transfers between devices  24.5 us (5%)
  other arithmetic  20.6 us (5%)
  between operations  14.3 us (3%)
  matrix products  9.18 us (2%)
    all_to_all x1, waiting for transfers between devices, on_device(): total = jnp.sum(lax.all_to_all(send, 'rep', 0, 0, tiled=True), axis=0)  139 us
    psum x1, waiting for transfers between devices, on_device(): coeff = lax.psum(own - total[rows:].reshape(rank, w_o + w_2) / n, 'shard')  115 us
    all_to_all x2, waiting for transfers between devices, gather_rep(): lax.all_to_all(jnp.broadcast_to(y[None], (n,) + y.shape), 'rep', 0, 0, ti...  69.6 us
    unnamed x39, local copies, waits for them, and re-layouts  22.1 us
    all_to_all x2, starting transfers between devices, gather_rep(): lax.all_to_all(jnp.broadcast_to(y[None], (n,) + y.shape), 'rep', 0, 0, ti...  17.2 us
    concatenate x1, local copies, waits for them, and re-layouts, on_device(): send = jnp.concatenate([dense, coef_part.reshape(n, -1, width)], axis=1)  14.7 us
    concatenate x1, other arithmetic, on_device(): send = jnp.concatenate([dense, coef_part.reshape(n, -1, width)], axis=1)  10.6 us
  transfers between devices with their start and end apart: 4, of which 4 were waited for; matrix products, arithmetic and copies ran while one was open for 4% of the time, Pallas kernels for 0%

commit v1 on v0

--- a/solution.py
+++ b/solution.py
@@ -81,7 +81,9 @@
     total = jnp.sum(lax.all_to_all(send, "rep", 0, 0, tiled=True), axis=0)
     summed = total[:rows]
     own = jnp.concatenate([project(basis_wo, outer_wo), project(basis_w2, outer_w2)], axis=1)
-    coeff = lax.psum(own - total[rows:].reshape(rank, w_o + w_2) / n, "shard")
+    coeff = jnp.sum(
+        lax.all_gather(own - total[rows:].reshape(rank, w_o + w_2) / n, "shard"), axis=0
+    )
     d_qkv = outer_wqkv - summed[:, :w_qkv] / n
     d_one = outer_w1 - summed[:, w_qkv : w_qkv + w_ff] / n
     d_three = outer_w3 - summed[:, w_qkv + w_ff :] / n

time: 457 us -> 339 us (0.74)
  waiting for transfers between devices: 323 us -> 198 us
  local copies, waits for them, and re-layouts: 63.8 us -> 71.4 us
    psum x1 -> x0, waiting for transfers between devices: 115 us -> none  [on_device(): coeff = lax.psum(own - total[rows:].reshape(rank, w_o + w_2) / n, 'shard')]
    all_to_all x2, waiting for transfers between devices: 69.6 us -> 6.06 us  [gather_rep(): lax.all_to_all(jnp.broadcast_to(y[None], (n,) + y.shape), 'rep', 0, 0, ti...]
    all_gather x0 -> x1, waiting for transfers between devices: none -> 52.3 us  [on_device(): lax.all_gather(own - total[rows:].reshape(rank, w_o + w_2) / n, 'shard')]
    unnamed x39 -> x41, local copies, waits for them, and re-layouts: 22.1 us -> 29.1 us
  transfers between devices with their start and end apart: 4 -> 4, of which waited for: 4 -> 3; matrix products, arithmetic and copies ran while one was open for 4% -> 11% of each run, Pallas kernels for 0% -> 0%
where the time goes in v1:
time: 339 us; the launch traced here: 335 us
  waiting for transfers between devices  198 us (58%)
  local copies, waits for them, and re-layouts  71.4 us (21%)
  starting transfers between devices  22.6 us (7%)
  other arithmetic  22.1 us (7%)
  between operations  14.3 us (4%)
  matrix products  6.86 us (2%)
    all_to_all x1, waiting for transfers between devices, on_device(): total = jnp.sum(lax.all_to_all(send, 'rep', 0, 0, tiled=True), axis=0)  139 us
    all_gather x1, waiting for transfers between devices, on_device(): lax.all_gather(own - total[rows:].reshape(rank, w_o + w_2) / n, 'shard')  52.3 us
    unnamed x41, local copies, waits for them, and re-layouts  29.1 us
    all_to_all x2, starting transfers between devices, gather_rep(): lax.all_to_all(jnp.broadcast_to(y[None], (n,) + y.shape), 'rep', 0, 0, ti...  15.3 us
    concatenate x1, local copies, waits for them, and re-layouts, on_device(): send = jnp.concatenate([dense, coef_part.reshape(n, -1, width)], axis=1)  14.7 us
    concatenate x1, other arithmetic, on_device(): send = jnp.concatenate([dense, coef_part.reshape(n, -1, width)], axis=1)  10.6 us
    all_to_all x1, starting transfers between devices, on_device(): total = jnp.sum(lax.all_to_all(send, 'rep', 0, 0, tiled=True), axis=0)  7.31 us
  transfers between devices with their start and end apart: 4, of which 3 were waited for; matrix products, arithmetic and copies ran while one was open for 11% of the time, Pallas kernels for 0%

profile of v1, /device:TPU:126, one launch (start us, length us, event | category | flops | bytes accessed | tf_op | source)
XLA Modules:
  0.0 334.8 jit_solution(317004555107380983)
XLA Ops:
  7.2 2.4 copy.97
  9.6 2.5 copy.96
  12.2 3.2 convolution_bitcast_fusion
  15.4 1.2 convolution_bitcast_fusion.1
  16.8 0.5 reshape.102
  17.3 4.6 %copy.75 = f32[8,16,2048]{1,2,0:T(8,128)} copy(f32[8,16,2048]{2,1,0:T(8,128)S(1)} %reshape.102) | data formatting | bytes 2097152 | tf_op jit(solution)/shard_map/reshape | solution.py:80
  21.9 2.4 copy.71
  24.3 3.6 %copy.72 = f32[1,128,6144]{1,2,0:T(8,128)} copy(f32[1,128,6144]{2,1,0:T(8,128)} %param.19) | data formatting | bytes 6291456 | tf_op args[2]
  27.9 3.0 copy.70
  30.9 10.6 %pad_maximum_fusion = f32[8,144,2048]{1,2,0:T(8,128)} fusion(f32[8,16,2048]{1,2,0:T(8,128)} %copy.75, f32[8,128,768]{1,2,0:T(8,128)} %bitcast.59, f32[8,128,768]{1,2,0:T(8,128)S(1)} %bitcast.58, f32[8,128,512]{1,2,0:T(8,128)} %bitcast.61), kind=kLoop, calls=%fused_computation | loop fusion | flops 7077888 | bytes 18874368 | tf_op jit(solution)/shard_map/concatenate | solution.py:80
  41.4 14.7 %copy.76 = f32[8,144,2048]{2,1,0:T(8,128)} copy(f32[8,144,2048]{1,2,0:T(8,128)} %pad_maximum_fusion) | data formatting | bytes 18874368 | tf_op jit(solution)/shard_map/concatenate | solution.py:80
  56.2 7.3 %all-to-all-start = ((f32[8,144,2048]{2,1,0:T(8,128)}), f32[8,144,2048]{2,1,0:T(8,128)}, u32[]{:S(2)}, u32[]{:S(2)}) async-start(f32[8,144,2048]{2,1,0:T(8,128)} %copy.76), calls=%async_computation | async-start | bytes 18874368 | tf_op jit(solution)/shard_map/all_to_all | solution.py:81
  63.5 0.2 convolution_bitcast_fusion.4
  63.7 0.3 convolution_bitcast_fusion.5
  64.1 139.2 %all-to-all-done = f32[8,144,2048]{2,1,0:T(8,128)} async-done(((f32[8,144,2048]{2,1,0:T(8,128)}), f32[8,144,2048]{2,1,0:T(8,128)}, u32[]{:S(2)}, u32[]{:S(2)}) %all-to-all-start) | async-done | bytes 9437216 | tf_op jit(solution)/shard_map/all_to_all | solution.py:81
  203.3 4.7 %reduce_sum.18 = f32[144,2048]{1,0:T(8,128)S(1)} reduce(f32[8,144,2048]{2,1,0:T(8,128)} %all-to-all-done, f32[]{:T(128)} %constant.4.clone.1), dimensions={0}, to_apply=%region_0.0 | reduce | flops 2064384 | bytes 10616836 | tf_op jit(solution)/shard_map/reduce_sum | solution.py:81
  208.1 0.7 maximum_subtract_fusion
  208.8 1.9 fusion.9
  210.7 2.3 fusion.10
  213.0 2.5 broadcast_in_dim.4
  215.5 7.0 %all-to-all-start.1 = ((bf16[8,128,2048]{2,1,0:T(8,128)(2,1)}), bf16[8,128,2048]{2,1,0:T(8,128)(2,1)}, u32[]{:S(2)}, u32[]{:S(2)}) async-start(bf16[8,128,2048]{2,1,0:T(8,128)(2,1)} %broadcast_in_dim.4), calls=%async_computation.1 | async-start | bytes 8388608 | tf_op jit(solution)/shard_map/all_to_all | solution.py:43
  222.6 0.2 copy.83
  222.8 0.2 copy.82
  223.1 52.3 %all-gather.2.cloned.1.call-done = f32[16,64,512]{2,1,0:T(8,128)} async-done(((f32[1,64,512]{2,1,0:T(8,128)}), f32[16,64,512]{2,1,0:T(8,128)}) %all-gather.2.cloned.1.call-update) | async-done | bytes 2097168 | tf_op jit(solution)/shard_map/all_gather | solution.py:85
  275.4 1.8 reduce_sum.19
  277.1 1.5 fusion.8
  278.6 0.1 copy.84
  278.9 0.4 fusion.7
  279.4 1.6 broadcast_in_dim.5
  281.0 8.2 %all-to-all-start.2 = ((bf16[8,128,1024]{2,1,0:T(8,128)(2,1)}), bf16[8,128,1024]{2,1,0:T(8,128)(2,1)S(1)}, u32[]{:S(2)}, u32[]{:S(2)}) async-start(bf16[8,128,1024]{2,1,0:T(8,128)(2,1)} %broadcast_in_dim.5), calls=%async_computation.2 | async-start | bytes 4194304 | tf_op jit(solution)/shard_map/all_to_all | solution.py:43
  289.3 3.8 %fusion.12 = (bf16[8,128,768]{2,1,0:T(8,128)(2,1)}, bf16[8,128,768]{2,1,0:T(8,128)(2,1)}) fusion(bf16[8,128,2048]{2,1,0:T(8,128)(2,1)} %all-to-all-done.1), kind=kLoop, calls=%fused_computation.37 | loop fusion | bytes 6291456 | tf_op jit(solution)/shard_map/slice | solution.py:101
  293.1 2.6 copy.99
  295.7 2.6 copy.89
  298.2 2.6 copy.100
  300.8 2.6 copy.90
  303.4 1.3 slice.51
  304.7 1.3 copy.98
  306.0 2.3 copy.88
  308.3 1.9 copy.93
  310.3 0.9 copy.95
  311.2 0.8 copy.92
  311.9 0.8 copy.94
  312.7 6.1 %all-to-all-done.2 = bf16[8,128,1024]{2,1,0:T(8,128)(2,1)S(1)} async-done(((bf16[8,128,1024]{2,1,0:T(8,128)(2,1)}), bf16[8,128,1024]{2,1,0:T(8,128)(2,1)S(1)}, u32[]{:S(2)}, u32[]{:S(2)}) %all-to-all-start.2) | async-done | bytes 2097184 | tf_op jit(solution)/shard_map/all_to_all | solution.py:43
  318.7 1.3 slice.58
  320.0 3.8 %reshape.108 = bf16[8,384,256]{2,1,0:T(8,128)(2,1)} reshape(bf16[8,128,768]{2,1,0:T(8,128)(2,1)} %slice.58) | data formatting | bytes 3145728 | tf_op jit(solution)/shard_map/reshape | solution.py:103
  323.8 2.8 copy.102
  326.6 0.3 copy.101
  326.9 1.0 copy.91
  (35 shorter events, 0.8 us)
Async XLA Ops:
  7.2 5.0 %copy-start = (f32[384,64]{0,1:T(8,128)S(1)}, f32[384,64]{0,1:T(8,128)}, u32[]{:S(2)}) copy-start(f32[384,64]{0,1:T(8,128)} %param.33) | copy-start | bytes 294916
  9.6 5.8 %copy-start.9 = (f32[128,64]{0,1:T(8,128)S(1)}, f32[128,64]{0,1:T(8,128)}, u32[]{:S(2)}) copy-start(f32[128,64]{0,1:T(8,128)} %param.32) | copy-start | bytes 98308
  12.2 3.2 copy-start.1
  56.2 7.3 %copy-start.4 = (f32[128,256]{1,0:T(8,128)S(1)}, f32[128,256]{1,0:T(8,128)}, u32[]{:S(2)}) copy-start(f32[128,256]{1,0:T(8,128)} %param.25) | copy-start | bytes 393220
  56.2 7.5 %copy-start.2 = (f32[384,256]{1,0:T(8,128)S(1)}, f32[384,256]{1,0:T(8,128)}, u32[]{:S(2)}) copy-start(f32[384,256]{1,0:T(8,128)} %param.26) | copy-start | bytes 1179652
  56.2 147.1 %all-to-all-start = ((f32[8,144,2048]{2,1,0:T(8,128)}), f32[8,144,2048]{2,1,0:T(8,128)}, u32[]{:S(2)}, u32[]{:S(2)}) async-start(f32[8,144,2048]{2,1,0:T(8,128)} %copy.76), calls=%async_computation | async-start | bytes 18874368 | tf_op jit(solution)/shard_map/all_to_all | solution.py:81
  63.5 211.9 %all-gather.2.cloned.1.call-start = ((), (), s32[]{:S(2)}) async-start(), calls=%async_computation.3 | async-start | bytes 2228224 | tf_op jit(solution)/shard_map/all_gather | solution.py:85
  64.1 146.6 %copy-start.5 = (f32[128,768]{1,0:T(8,128)S(1)}, f32[128,768]{1,0:T(8,128)}, u32[]{:S(2)}) copy-start(f32[128,768]{1,0:T(8,128)} %param.23) | copy-start | bytes 1179652
  64.1 146.6 %copy-start.6 = (f32[128,768]{1,0:T(8,128)S(1)}, f32[128,768]{1,0:T(8,128)}, u32[]{:S(2)}) copy-start(f32[128,768]{1,0:T(8,128)} %param.28) | copy-start | bytes 1179652
  64.1 146.6 %copy-start.7 = (f32[128,768]{1,0:T(8,128)S(1)}, f32[128,768]{1,0:T(8,128)}, u32[]{:S(2)}) copy-start(f32[128,768]{1,0:T(8,128)} %param.24) | copy-start | bytes 1179652
  215.5 7.3 %copy-start.8 = (f32[384,256]{1,0:T(8,128)S(1)}, f32[384,256]{1,0:T(8,128)}, u32[]{:S(2)}) copy-start(f32[384,256]{1,0:T(8,128)} %param.31) | copy-start | bytes 1179652
  215.5 7.5 %copy-start.10 = (f32[128,256]{1,0:T(8,128)S(1)}, f32[128,256]{1,0:T(8,128)}, u32[]{:S(2)}) copy-start(f32[128,256]{1,0:T(8,128)} %param.30) | copy-start | bytes 393220
  215.5 63.9 %all-to-all-start.1 = ((bf16[8,128,2048]{2,1,0:T(8,128)(2,1)}), bf16[8,128,2048]{2,1,0:T(8,128)(2,1)}, u32[]{:S(2)}, u32[]{:S(2)}) async-start(bf16[8,128,2048]{2,1,0:T(8,128)(2,1)} %broadcast_in_dim.4), calls=%async_computation.1 | async-start | bytes 8388608 | tf_op jit(solution)/shard_map/all_to_all | solution.py:43
  281.0 37.7 %all-to-all-start.2 = ((bf16[8,128,1024]{2,1,0:T(8,128)(2,1)}), bf16[8,128,1024]{2,1,0:T(8,128)(2,1)S(1)}, u32[]{:S(2)}, u32[]{:S(2)}) async-start(bf16[8,128,1024]{2,1,0:T(8,128)(2,1)} %broadcast_in_dim.5), calls=%async_computation.2 | async-start | bytes 4194304 | tf_op jit(solution)/shard_map/all_to_all | solution.py:43
  306.0 4.2 %copy-start.3 = (f32[384,256]{0,1:T(8,128)S(1)}, f32[384,256]{0,1:T(8,128)}, u32[]{:S(2)}) copy-start(f32[384,256]{0,1:T(8,128)} %get-tuple-element.93) | copy-start | bytes 1179652
Sparse Core Ops, SparseCore 0:
  208.9 66.4 all-gather.1
